TPU v7x, 32 devices: a whole 2x2x4 slice. The times are simulated.
32 devices in a mesh: grp: 4 (over x, core), tp: 8 (over z, y).
Axes of the slice: x: 2, y: 2, z: 4, core: 2. Of those that a mesh axis runs over, the one named last changes fastest.
Arguments:
- hidden_in: bfloat16 [3072, 3584], P('grp'), may hold values from -6 to 6
- lengths: int32 [8, 8], P('grp'), may hold values from 1 to 96, 384 in all within a row
- dest: int32 [64, 1], P('grp'), may hold values from 0 to 3; in each aligned block of 16 rows (0 to 15, 16 to 31, ...) at most 4 rows name the same one
- attn_gain: float32 [3584], replicated, may hold values from 0.6 to 8
- q_weight: bfloat16 [3584, 2048], P('grp', 'tp'), may hold values from -0.09375 to 0.09375
- k_weight: bfloat16 [3584, 512], P('grp', 'tp'), may hold values from -0.09375 to 0.09375
- v_weight: bfloat16 [3584, 512], P('grp', 'tp'), may hold values from -0.09375 to 0.09375
- o_weight: bfloat16 [3584, 2048], P('grp', 'tp'), may hold values from -0.125 to 0.125
- ffn_gain: float32 [3584], replicated, may hold values from 0.1 to 1.9
- gate_weight: bfloat16 [3584, 10240], P('grp', 'tp'), may hold values from -0.09375 to 0.09375
- up_weight: bfloat16 [3584, 10240], P('grp', 'tp'), may hold values from -0.09375 to 0.09375
- down_weight: bfloat16 [3584, 10240], P('grp', 'tp'), may hold values from -0.0625 to 0.0625
Outputs:
- bank_in: bfloat16 [4, 4, 4, 3584], P('grp', None, None, 'tp')
Inputs may be any that keep to these rules, and one draw needn't show every extreme that they name: Each block's 8 lengths sum to 384. `dest`: among the programs of one index of grp, no bank shard is named by more than 4.
All inputs are finite; a program needn't handle non-finite values.
Results may differ from a plain program's by a relative error of at most 0.015.
The roundings to bfloat16 on the way count: a program that leaves them out, or rounds other values in their place, can miss the bound.
Values may be sent and summed in bfloat16 or wider, within the bound.
No kernel may reach another device: no remote copies, remote signals or barrier semaphores. Data moves between devices by JAX's collectives and lax.ppermute only.
A program may use at most 128 MiB of HBM per device.

v0:
```python
import jax
import jax.numpy as jnp
from jax import lax
from jax.sharding import PartitionSpec as P

HEAD_SIZE = 128
KVH = 4
HEADS = 16
EPSILON = 1e-06
HIGH = lax.Precision.HIGHEST


def rms_scale(rows, gain):
    rows = rows.astype(jnp.float32)
    factor = lax.rsqrt(jnp.mean(rows * rows, axis=1, keepdims=True) + EPSILON)
    return (rows * factor * gain[None, :]).astype(jnp.bfloat16)


def segment_ids(lengths, block_rows):
    bounds = jnp.cumsum(lengths, axis=1)
    position = lax.broadcasted_iota(jnp.int32, (lengths.shape[0], block_rows), 1)
    return jnp.sum((position[:, :, None] >= bounds[:, None, :]).astype(jnp.int32), axis=2)


def softmax_rows(attention_scores):
    top = jnp.max(attention_scores, axis=-1, keepdims=True)
    expo = jnp.exp(attention_scores - top)
    return (expo / jnp.sum(expo, axis=-1, keepdims=True)).astype(jnp.bfloat16)


def transposed_dot(left, right):
    return lax.dot_general(
        left, right, (((1,), (1,)), ((), ())), preferred_element_type=jnp.float32
    )


def on_device(
    hidden_in,
    lengths,
    dest,
    attn_gain,
    q_weight,
    k_weight,
    v_weight,
    o_weight,
    ffn_gain,
    gate_weight,
    up_weight,
    down_weight,
):
    row_count, width = hidden_in.shape
    blocks, per_block = lengths.shape
    block_rows = row_count // blocks
    programs = blocks * per_block
    tp_size = lax.axis_size("tp")
    grp_size = lax.axis_size("grp")
    local_heads = q_weight.shape[1] // HEAD_SIZE
    norm_in = rms_scale(hidden_in, attn_gain)
    q_full, k_full, v_full, o_full, gate_full, up_full, down_full = (
        lax.all_gather(q_weight, "grp", axis=0, tiled=True),
        lax.all_gather(k_weight, "grp", axis=0, tiled=True),
        lax.all_gather(v_weight, "grp", axis=0, tiled=True),
        lax.all_gather(o_weight, "grp", axis=0, tiled=True),
        lax.all_gather(gate_weight, "grp", axis=0, tiled=True),
        lax.all_gather(up_weight, "grp", axis=0, tiled=True),
        lax.all_gather(down_weight, "grp", axis=0, tiled=True),
    )
    queries = jnp.dot(norm_in, q_full, preferred_element_type=jnp.float32).astype(jnp.bfloat16)
    key_part = jnp.dot(norm_in, k_full, preferred_element_type=jnp.float32).astype(jnp.bfloat16)
    value_part = jnp.dot(norm_in, v_full, preferred_element_type=jnp.float32).astype(jnp.bfloat16)
    keys_all, vals_all = (
        lax.all_gather(key_part, "tp", axis=1, tiled=True),
        lax.all_gather(value_part, "tp", axis=1, tiled=True),
    )
    kv_count = keys_all.shape[1] // HEAD_SIZE
    kv_index = lax.axis_index("tp") * local_heads // (HEADS // KVH)
    key_head = lax.dynamic_slice_in_dim(
        keys_all.reshape(row_count, HEAD_SIZE, kv_count), kv_index, 1, 2
    )[:, :, 0]
    value_head = lax.dynamic_slice_in_dim(
        vals_all.reshape(row_count, HEAD_SIZE, kv_count), kv_index, 1, 2
    )[:, :, 0]
    segs = segment_ids(lengths, block_rows)
    same = segs[:, :, None] == segs[:, None, :]
    blocked_queries = queries.reshape(blocks, block_rows, local_heads, HEAD_SIZE)
    blocked_keys = key_head.reshape(blocks, block_rows, HEAD_SIZE)
    blocked_values = value_head.reshape(blocks, block_rows, HEAD_SIZE)
    attention_scores = jnp.einsum(
        "xwre,xpe->xrwp", blocked_queries, blocked_keys, preferred_element_type=jnp.float32
    ) * HEAD_SIZE ** (-0.5)
    attention_scores = jnp.where(same[:, None, :, :], attention_scores, -1e30)
    attention_probabilities = softmax_rows(attention_scores)
    attended_rows = jnp.einsum(
        "asfo,aon->afsn",
        attention_probabilities,
        blocked_values,
        preferred_element_type=jnp.float32,
    )
    attended_rows = attended_rows.astype(jnp.bfloat16).reshape(row_count, local_heads * HEAD_SIZE)
    attn_term = transposed_dot(attended_rows, o_full)
    attn_total = lax.psum(attn_term.astype(jnp.bfloat16), "tp").astype(jnp.float32)
    residual = hidden_in.astype(jnp.float32) + attn_total
    norm_mid = rms_scale(residual, ffn_gain)
    gate_pre = jnp.dot(norm_mid, gate_full, preferred_element_type=jnp.float32)
    up_pre = jnp.dot(norm_mid, up_full, preferred_element_type=jnp.float32)
    hidden_ffn = (jax.nn.silu(gate_pre) * up_pre).astype(jnp.bfloat16)
    ffn_term = transposed_dot(hidden_ffn, down_full)
    share = row_count // tp_size
    tp_index = lax.axis_index("tp")
    block_index = lax.broadcasted_iota(jnp.int32, (blocks, block_rows), 0)
    program_of_row = (block_index * per_block + segs).reshape(row_count)
    program_grid = lax.broadcasted_iota(jnp.int32, (programs, row_count), 0)
    selector = program_grid == program_of_row[None, :]
    selector_float = selector.astype(jnp.float32)
    residual_share = lax.dynamic_slice_in_dim(residual, tp_index * share, share, 0)
    selector_share = lax.dynamic_slice_in_dim(selector_float, tp_index * share, share, 1)
    ffn_share = lax.psum_scatter(
        ffn_term.astype(jnp.bfloat16), "tp", scatter_dimension=0, tiled=True
    ).astype(jnp.float32)
    pooled_part = jnp.dot(
        selector_share,
        residual_share + ffn_share,
        precision=HIGH,
        preferred_element_type=jnp.float32,
    )
    pooled_sums = lax.psum_scatter(
        pooled_part.astype(jnp.bfloat16), "tp", scatter_dimension=1, tiled=True
    ).astype(jnp.float32)
    counts = lengths.reshape(programs).astype(jnp.float32)
    embedded = (pooled_sums / counts[:, None]).astype(jnp.bfloat16)
    capacity = max(2, (programs + grp_size - 1) // grp_size)
    targets = dest[:, 0]
    grp_ids = lax.broadcasted_iota(jnp.int32, (programs, grp_size), 1)
    chosen = (targets[:, None] == grp_ids).astype(jnp.int32)
    earlier = jnp.cumsum(chosen, axis=0) - chosen
    slot_rank = jnp.sum(earlier * chosen, axis=1)
    slot_ids = targets * capacity + slot_rank
    slot_grid = lax.broadcasted_iota(jnp.int32, (grp_size * capacity, programs), 0)
    placer = (slot_grid == slot_ids[None, :]).astype(jnp.bfloat16)
    outgoing = jnp.dot(placer, embedded, preferred_element_type=jnp.float32).astype(jnp.bfloat16)
    outgoing = outgoing.reshape(grp_size, capacity, embedded.shape[1])
    incoming = lax.all_to_all(outgoing, "grp", split_axis=0, concat_axis=0, tiled=True)
    return incoming.reshape(1, grp_size, capacity, embedded.shape[1])


def solution(mesh):
    placed = (
        P("grp", None),
        P("grp", None),
        P("grp", None),
        P(),
        P("grp", "tp"),
        P("grp", "tp"),
        P("grp", "tp"),
        P("grp", "tp"),
        P(),
        P("grp", "tp"),
        P("grp", "tp"),
        P("grp", "tp"),
    )
    return jax.shard_map(
        on_device, mesh=mesh, in_specs=placed, out_specs=P("grp", None, None, "tp"), check_vma=False
    )
```

profile of v0, /device:TPU:0, one launch (start us, length us, event | category | flops | bytes accessed | tf_op | source)
XLA Modules:
  0.0 716.7 jit_solution(17084657934199434864)
XLA Ops:
  6.5 0.7 all-gather.6.cloned.1.call-update
  7.3 0.7 all-gather.8.cloned.1.call-update
  8.1 3.9 fusion.1
  11.9 8.3 %all_gather.27 = bf16[3584,64]{0,1:T(8,128)(2,1)S(1)} all-gather(bf16[896,64]{0,1:T(8,128)(2,1)S(1)} %copy-done.2), channel_id=1, replica_groups=mesh['grp'=4,'tp'=8] {'grp'}, dimensions={0}, use_global_device_ids=true | all-gather | bytes 573440 | tf_op jit(solution)/shard_map/all_gather | solution.py:62
  20.2 2.2 fusion.3
  22.4 2.4 copy-done.1
  24.8 1.8 convolution_convert_fusion.6
  26.6 32.6 %all_gather.28 = bf16[768,512]{0,1:T(8,128)(2,1)S(1)} all-gather(bf16[768,64]{0,1:T(8,128)(2,1)S(1)} %convolution_convert_fusion.6), channel_id=1, replica_groups=mesh['grp'=4,'tp'=8] {'tp'}, dimensions={1}, use_global_device_ids=true | all-gather | bytes 884736 | tf_op jit(solution)/shard_map/all_gather | solution.py:73
  59.4 6.5 all_gather.29
  65.9 4.3 convolution_convert_fusion.5
  70.2 32.1 %all_gather.30 = bf16[768,512]{0,1:T(8,128)(2,1)S(1)} all-gather(bf16[768,64]{0,1:T(8,128)(2,1)S(1)} %convolution_convert_fusion.5), channel_id=1, replica_groups=mesh['grp'=4,'tp'=8] {'tp'}, dimensions={1}, use_global_device_ids=true | all-gather | bytes 884736 | tf_op jit(solution)/shard_map/all_gather | solution.py:72
  102.4 0.8 constant_dynamic-slice_fusion
  104.6 4.7 convolution_convert_fusion.4
  109.5 2.4 fusion.32
  111.8 2.1 fusion.9
  114.4 5.5 convolution_convert_fusion.1
  119.9 0.5 all-gather.10.cloned.1.call-update
  120.5 0.5 all-gather.12.cloned.1.call-update
  121.7 189.5 %all-reduce.2.cloned.1.call-done = bf16[768,3584]{1,0:T(8,128)(2,1)} async-done(((bf16[768,3584]{1,0:T(8,128)(2,1)}), bf16[768,3584]{1,0:T(8,128)(2,1)}) %all-reduce.2.cloned.1.call-update) | async-done | bytes 5505040 | tf_op jit(solution)/shard_map/psum | solution.py:101
  311.2 11.4 %convert_add_fusion = (f32[768,3584]{1,0:T(8,128)}, f32[768]{0:T(1024)S(1)}) fusion(bf16[768,3584]{1,0:T(8,128)(2,1)} %param.12, bf16[768,3584]{1,0:T(8,128)(2,1)} %all-reduce.2.cloned.1.call-done), kind=kLoop, calls=%fused_computation.1 | loop fusion | flops 13761792 | bytes 22023168 | tf_op jit(solution)/shard_map/add | solution.py:102
  322.6 51.9 %all-gather.10.cloned.1.call-done = bf16[3584,1280]{1,0:T(8,128)(2,1)} async-done(((bf16[896,1280]{1,0:T(8,128)(2,1)}), bf16[3584,1280]{1,0:T(8,128)(2,1)}) %all-gather.10.cloned.1.call-update) | async-done | bytes 9175056 | tf_op jit(solution)/shard_map/all_gather | solution.py:64
  374.5 14.7 %fusion.31 = f32[768,1280]{1,0:T(8,128)} fusion(bf16[3584,1280]{1,0:T(8,128)(2,1)} %all-gather.10.cloned.1.call-done, f32[3584]{0:T(1024)S(1)} %copy-done.7, f32[768]{0:T(1024)S(1)} %add_rsqrt_fusion, bf16[768,3584]{1,0:T(8,128)(2,1)} %param.12, bf16[768,3584]{1,0:T(8,128)(2,1)} %all-reduce.2.cloned.1.call-done), kind=kOutput, calls=%fused_computation.57 | convolution fusion | flops 7062945792 | bytes 24134656 | tf_op jit(solution)/shard_map/dot_general | solution.py:104
  389.1 49.6 %all-gather.12.cloned.1.call-done = bf16[3584,1280]{1,0:T(8,128)(2,1)} async-done(((bf16[896,1280]{1,0:T(8,128)(2,1)}), bf16[3584,1280]{1,0:T(8,128)(2,1)}) %all-gather.12.cloned.1.call-update) | async-done | bytes 9175056 | tf_op jit(solution)/shard_map/all_gather | solution.py:65
  438.7 64.3 %all-gather.14.cloned.1.call-done = bf16[3584,1280]{1,0:T(8,128)(2,1)} async-done(((bf16[896,1280]{1,0:T(8,128)(2,1)}), bf16[3584,1280]{1,0:T(8,128)(2,1)}) %all-gather.14.cloned.1.call-update) | async-done | bytes 9175056 | tf_op jit(solution)/shard_map/all_gather | solution.py:66
  503.0 25.9 %convolution_convert_fusion = bf16[768,3584]{1,0:T(8,128)(2,1)} fusion(bf16[3584,1280]{1,0:T(8,128)(2,1)} %all-gather.14.cloned.1.call-done, bf16[3584,1280]{1,0:T(8,128)(2,1)} %all-gather.12.cloned.1.call-done, f32[768,1280]{1,0:T(8,128)} %fusion.31, f32[3584]{0:T(1024)S(1)} %copy-done.7, f32[768]{0:T(1024)S(1)} %add_rsqrt_fusion, ...), kind=kOutput, calls=%fused_computation.9 | convolution fusion | flops 14118027264 | bytes 38814720 | tf_op jit(solution)/shard_map/dot_general | solution.py:32
  529.8 105.6 %reduce-scatter.5.cloned.1.call-done = bf16[96,3584]{1,0:T(8,128)(2,1)} async-done(((bf16[768,3584]{1,0:T(8,128)(2,1)}), bf16[96,3584]{1,0:T(8,128)(2,1)}) %reduce-scatter.5.cloned.1.call-update) | async-done | bytes 688144 | tf_op jit(solution)/shard_map/reduce_scatter | solution.py:117
  635.4 2.2 convolution_convert_fusion.2
  637.6 1.2 copy.39
  639.1 62.5 %reduce-scatter.7.cloned.1.call-done = bf16[448,16]{1,0:T(8,128)(2,1)} async-done(((bf16[3584,16]{1,0:T(8,128)(2,1)}), bf16[448,16]{1,0:T(8,128)(2,1)}) %reduce-scatter.7.cloned.1.call-update) | async-done | bytes 14352
  701.6 1.0 copy.40
  702.8 6.4 all_to_all.5
  709.2 0.6 copy.59
  (52 shorter events, 4.4 us)
Async XLA Ops:
  6.5 5.4 copy-start.2
  6.5 13.7 %copy-start.4 = (f32[3584]{0:T(1024)S(1)}, f32[3584]{0:T(1024)}, u32[]{:S(2)}) copy-start(f32[3584]{0:T(1024)} %param.15) | copy-start | bytes 43012
  6.5 98.1 %all-gather.6.cloned.1.call-start = ((), (), s32[]{:S(2)}) async-start(), calls=%async_computation.3 | async-start | bytes 2293760 | tf_op jit(solution)/shard_map/all_gather | solution.py:60
  7.3 107.1 %all-gather.8.cloned.1.call-start = ((), (), s32[]{:S(2)}) async-start(), calls=%async_computation.4 | async-start | bytes 2293760 | tf_op jit(solution)/shard_map/all_gather | solution.py:63
  8.0 303.2 %all-reduce.2.cloned.1.call-start = ((), (), s32[]{:S(2)}) async-start(), calls=%async_computation.5 | async-start | bytes 11010048 | tf_op jit(solution)/shard_map/psum | solution.py:101
  8.1 12.2 %copy-start = (bf16[768,3584]{1,0:T(8,128)(2,1)S(1)}, bf16[768,3584]{1,0:T(8,128)(2,1)}, u32[]{:S(2)}) copy-start(bf16[768,3584]{1,0:T(8,128)(2,1)} %param.12) | copy-start | bytes 16515076
  22.4 2.4 copy-start.1
  24.8 34.5 %copy-start.3 = (bf16[896,64]{0,1:T(8,128)(2,1)S(1)}, bf16[896,64]{0,1:T(8,128)(2,1)}, u32[]{:S(2)}) copy-start(bf16[896,64]{0,1:T(8,128)(2,1)} %param.17) | copy-start | bytes 344068
  59.3 44.3 %copy-start.5 = (s32[2,8]{1,0:T(2,128)S(1)}, s32[2,8]{1,0:T(2,128)}, u32[]{:S(2)}) copy-start(s32[2,8]{1,0:T(2,128)} %param.13) | copy-start | bytes 196
  119.9 254.6 %all-gather.10.cloned.1.call-start = ((), (), s32[]{:S(2)}) async-start(), calls=%async_computation.6 | async-start | bytes 11468800 | tf_op jit(solution)/shard_map/all_gather | solution.py:64
  120.5 318.2 %all-gather.12.cloned.1.call-start = ((), (), s32[]{:S(2)}) async-start(), calls=%async_computation.7 | async-start | bytes 11468800 | tf_op jit(solution)/shard_map/all_gather | solution.py:65
  121.1 381.9 %all-gather.14.cloned.1.call-start = ((), (), s32[]{:S(2)}) async-start(), calls=%async_computation.8 | async-start | bytes 11468800 | tf_op jit(solution)/shard_map/all_gather | solution.py:66
  121.6 252.8 %copy-start.7 = (f32[3584]{0:T(1024)S(1)}, f32[3584]{0:T(1024)}, u32[]{:S(2)}) copy-start(f32[3584]{0:T(1024)} %param.20) | copy-start | bytes 43012
  121.7 513.7 %reduce-scatter.5.cloned.1.call-start = ((), (), s32[]{:S(2)}) async-start(), calls=%async_computation.9 | async-start | bytes 6193152 | tf_op jit(solution)/shard_map/reduce_scatter | solution.py:117
  528.9 0.7 copy-start.6
  529.0 172.7 %reduce-scatter.7.cloned.1.call-start = ((), (), s32[]{:S(2)}) async-start(), calls=%async_computation.10 | async-start | bytes 1032192
Sparse Core Ops, SparseCore 0:
  8.9 23.8 all-gather.5
  34.3 21.1 all-gather.7
  120.0 191.1 all-reduce.1
  312.7 61.7 all-gather.9
  375.9 62.7 all-gather.11
  440.2 62.7 all-gather.13
  529.1 106.2 reduce-scatter.4
  639.0 62.6 reduce-scatter.6
where the time goes:
time: 717 us
  waiting for transfers between devices  526 us (73%)
  blocking collectives  85.8 us (12%)
  matrix products  63.7 us (9%)
  other arithmetic  18.3 us (3%)
  between operations  13.7 us (2%)
  local copies, waits for them, and re-layouts  8.39 us (1%)
    psum x1, waiting for transfers between devices, on_device(): lax.psum(attn_term.astype(jnp.bfloat16), 'tp').astype(jnp.float32)  189 us
    reduce_scatter x1, waiting for transfers between devices, on_device(): lax.psum_scatter(ffn_term.astype(jnp.bfloat16), 'tp', scatter_dimension=0...  106 us
    unnamed x9, waiting for transfers between devices  65.4 us
    all_gather x1, waiting for transfers between devices, on_device(): lax.all_gather(down_weight, 'grp', axis=0, tiled=True)  64.3 us
    all_gather x1, waiting for transfers between devices, on_device(): lax.all_gather(gate_weight, 'grp', axis=0, tiled=True)  51.9 us
    all_gather x1, waiting for transfers between devices, on_device(): lax.all_gather(up_weight, 'grp', axis=0, tiled=True)  49.6 us
    all_gather x1, blocking collectives, on_device(): lax.all_gather(value_part, 'tp', axis=1, tiled=True)  32.6 us
    all_gather x1, blocking collectives, on_device(): lax.all_gather(key_part, 'tp', axis=1, tiled=True)  32.1 us
  transfers between devices with their start and end apart: 8, of which 6 were waited for; matrix products, arithmetic and copies ran while one was open for 7% of the time, Pallas kernels for 0%

commit v1 on v0

--- a/solution.py
+++ b/solution.py
@@ -8,6 +8,29 @@
 HEADS = 16
 EPSILON = 1e-06
 HIGH = lax.Precision.HIGHEST
+
+
+def _post_columns(xin, dimension_no):
+    xin = jnp.moveaxis(xin, 0, dimension_no)
+    a_now = xin.shape
+    moved = xin.reshape(
+        *a_now[:dimension_no],
+        a_now[dimension_no] * a_now[dimension_no + 1],
+        *a_now[dimension_no + 2 :]
+    )
+    return moved
+
+
+def note_the_tracks(local_block, link_axis):
+    n_chips = lax.psum(1, link_axis)
+    reached = local_block[None]
+    for to_i in range(n_chips.bit_length() - 1):
+        outer = 1 << to_i
+        y2 = lax.ppermute(reached, link_axis, list(map(lambda s: (s, s ^ outer), range(n_chips))))
+        res = jnp.stack([reached, y2])
+        f_next = lax.axis_index(link_axis) >> to_i & 1
+        reached = jnp.where(f_next == 0, res, res[::-1]).reshape(-1, *local_block.shape)
+    return reached
 
 
 def rms_scale(rows, gain):
@@ -56,12 +79,18 @@
     grp_size = lax.axis_size("grp")
     local_heads = q_weight.shape[1] // HEAD_SIZE
     norm_in = rms_scale(hidden_in, attn_gain)
+
+    def _connect_wall(panel, a0, pos_dim):
+        b_next = note_the_tracks(panel, a0)
+        carry_out = _post_columns(b_next, pos_dim)
+        return carry_out
+
     q_full, k_full, v_full, o_full, gate_full, up_full, down_full = (
         lax.all_gather(q_weight, "grp", axis=0, tiled=True),
         lax.all_gather(k_weight, "grp", axis=0, tiled=True),
         lax.all_gather(v_weight, "grp", axis=0, tiled=True),
         lax.all_gather(o_weight, "grp", axis=0, tiled=True),
-        lax.all_gather(gate_weight, "grp", axis=0, tiled=True),
+        _connect_wall(gate_weight, "grp", 0),
         lax.all_gather(up_weight, "grp", axis=0, tiled=True),
         lax.all_gather(down_weight, "grp", axis=0, tiled=True),
     )

time: 717 us -> 653 us (0.911)
  waiting for transfers between devices: 526 us -> 433 us
  other arithmetic: 18.3 us -> 46.8 us
    psum x1, waiting for transfers between devices: 189 us -> 55.4 us  [on_device(): lax.psum(attn_term.astype(jnp.bfloat16), 'tp').astype(jnp.float32)]
    ppermute x0 -> x2, waiting for transfers between devices: none -> 105 us  [note_the_tracks(): lax.ppermute(reached, link_axis, list(map(lambda s: (s, s ^ outer), range...]
    all_gather x1 -> x0, waiting for transfers between devices: 51.9 us -> none  [on_device(): lax.all_gather(gate_weight, 'grp', axis=0, tiled=True)]
    all_gather x1, waiting for transfers between devices: 64.3 us -> 38.7 us  [on_device(): lax.all_gather(down_weight, 'grp', axis=0, tiled=True)]
    another operation x0 -> x3, other arithmetic: none -> 15.1 us  [note_the_tracks(): res = jnp.stack([reached, y2])]
    all_gather x1, waiting for transfers between devices: 49.6 us -> 64.3 us  [on_device(): lax.all_gather(up_weight, 'grp', axis=0, tiled=True)]
    select_n x0 -> x1, other arithmetic: none -> 13.2 us  [note_the_tracks(): jnp.where(f_next == 0, res, res[::-1]).reshape(-1, *local_block.shape)]
    unnamed x9 -> x8, waiting for transfers between devices: 65.4 us -> 64.9 us
  transfers between devices with their start and end apart: 8 -> 9, of which waited for: 6 -> 7; matrix products, arithmetic and copies ran while one was open for 7% -> 12% of each run, Pallas kernels for 0% -> 0%
where the time goes in v1:
time: 653 us
  waiting for transfers between devices  433 us (66%)
  blocking collectives  85.8 us (13%)
  matrix products  62 us (9%)
  other arithmetic  46.8 us (7%)
  between operations  13.7 us (2%)
  local copies, waits for them, and re-layouts  9.52 us (1%)
    reduce_scatter x1, waiting for transfers between devices, on_device(): lax.psum_scatter(ffn_term.astype(jnp.bfloat16), 'tp', scatter_dimension=0...  106 us
    ppermute x2, waiting for transfers between devices, note_the_tracks(): lax.ppermute(reached, link_axis, list(map(lambda s: (s, s ^ outer), range...  105 us
    unnamed x8, waiting for transfers between devices  64.9 us
    all_gather x1, waiting for transfers between devices, on_device(): lax.all_gather(up_weight, 'grp', axis=0, tiled=True)  64.3 us
    psum x1, waiting for transfers between devices, on_device(): lax.psum(attn_term.astype(jnp.bfloat16), 'tp').astype(jnp.float32)  55.4 us
    all_gather x1, waiting for transfers between devices, on_device(): lax.all_gather(down_weight, 'grp', axis=0, tiled=True)  38.7 us
    all_gather x1, blocking collectives, on_device(): lax.all_gather(value_part, 'tp', axis=1, tiled=True)  32.6 us
    all_gather x1, blocking collectives, on_device(): lax.all_gather(key_part, 'tp', axis=1, tiled=True)  32.1 us
  transfers between devices with their start and end apart: 9, of which 7 were waited for; matrix products, arithmetic and copies ran while one was open for 12% of the time, Pallas kernels for 0%

profile of v1, /device:TPU:0, one launch (start us, length us, event | category | flops | bytes accessed | tf_op | source)
XLA Modules:
  0.0 653.0 jit_solution(9011654634883844832)
XLA Ops:
  8.1 3.9 fusion.1
  11.9 8.3 %all_gather.24 = bf16[3584,64]{0,1:T(8,128)(2,1)S(1)} all-gather(bf16[896,64]{0,1:T(8,128)(2,1)S(1)} %copy-done.4), channel_id=1, replica_groups=mesh['grp'=4,'tp'=8] {'grp'}, dimensions={0}, use_global_device_ids=true | all-gather | bytes 573440 | tf_op jit(solution)/shard_map/all_gather | solution.py:91
  20.2 2.2 fusion.3
  22.4 2.4 copy-done.1
  24.8 1.8 convolution_convert_fusion.6
  26.6 32.6 %all_gather.25 = bf16[768,512]{0,1:T(8,128)(2,1)S(1)} all-gather(bf16[768,64]{0,1:T(8,128)(2,1)S(1)} %convolution_convert_fusion.6), channel_id=1, replica_groups=mesh['grp'=4,'tp'=8] {'tp'}, dimensions={1}, use_global_device_ids=true | all-gather | bytes 884736 | tf_op jit(solution)/shard_map/all_gather | solution.py:102
  59.4 6.5 all_gather.26
  65.9 4.3 convolution_convert_fusion.5
  70.2 32.1 %all_gather.27 = bf16[768,512]{0,1:T(8,128)(2,1)S(1)} all-gather(bf16[768,64]{0,1:T(8,128)(2,1)S(1)} %convolution_convert_fusion.5), channel_id=1, replica_groups=mesh['grp'=4,'tp'=8] {'tp'}, dimensions={1}, use_global_device_ids=true | all-gather | bytes 884736 | tf_op jit(solution)/shard_map/all_gather | solution.py:101
  105.2 4.7 convolution_convert_fusion.4
  110.0 2.3 fusion.34
  112.4 2.1 fusion.11
  114.9 5.5 convolution_convert_fusion.1
  122.1 4.6 collective-permute-done
  126.6 2.4 pad_maximum_fusion.1
  129.0 4.5 fusion.5
  133.5 1.4 collective-permute-start.1
  134.9 100.1 %collective-permute-done.1 = bf16[2,896,1280]{2,1,0:T(8,128)(2,1)} collective-permute-done((bf16[2,896,1280]{2,1,0:T(8,128)(2,1)}, bf16[2,896,1280]{2,1,0:T(8,128)(2,1)}, u32[]{:S(2)}, u32[]{:S(2)}) %collective-permute-start.1) | collective-permute-done | bytes 4587552 | tf_op jit(solution)/shard_map/ppermute | solution.py:29
  235.0 8.2 %pad_maximum_fusion = bf16[2,2,896,1280]{3,2,1,0:T(8,128)(2,1)} fusion(bf16[1,2,896,1280]{3,2,1,0:T(8,128)(2,1)} %bitcast.13, bf16[1,2,896,1280]{3,2,1,0:T(8,128)(2,1)} %get-tuple-element.7), kind=kLoop, calls=%fused_computation.10 | loop fusion | flops 4587520 | bytes 18350080 | tf_op jit(solution)/shard_map/stack | solution.py:30
  243.2 13.2 %reverse_select_fusion = bf16[2,2,896,1280]{3,2,1,0:T(8,128)(2,1)} fusion(bf16[2,2,896,1280]{3,2,1,0:T(8,128)(2,1)} %pad_maximum_fusion, pred[]{:T(512)S(6)} %eq.56), kind=kLoop, calls=%fused_computation.4 | loop fusion | flops 4587520 | bytes 18350080 | tf_op jit(solution)/shard_map/jit(_where)/select_n | solution.py:32
  256.4 55.4 %all-reduce.2.cloned.1.call-done = bf16[768,3584]{1,0:T(8,128)(2,1)} async-done(((bf16[768,3584]{1,0:T(8,128)(2,1)}), bf16[768,3584]{1,0:T(8,128)(2,1)}) %all-reduce.2.cloned.1.call-update) | async-done | bytes 5505040 | tf_op jit(solution)/shard_map/psum | solution.py:130
  311.7 11.6 %convert_add_fusion = (f32[768,3584]{1,0:T(8,128)}, f32[768]{0:T(1024)S(1)}) fusion(bf16[768,3584]{1,0:T(8,128)(2,1)} %param.12, bf16[768,3584]{1,0:T(8,128)(2,1)} %all-reduce.2.cloned.1.call-done), kind=kLoop, calls=%fused_computation.1 | loop fusion | flops 13761792 | bytes 22023168 | tf_op jit(solution)/shard_map/add | solution.py:131
  323.3 13.0 %fusion.33 = f32[768,1280]{1,0:T(8,128)} fusion(bf16[3584,1280]{1,0:T(8,128)(2,1)S(1)} %bitcast.54, f32[3584]{0:T(1024)S(1)} %copy-done.12, f32[768]{0:T(1024)S(1)} %add_rsqrt_fusion, bf16[768,3584]{1,0:T(8,128)(2,1)} %param.12, bf16[768,3584]{1,0:T(8,128)(2,1)} %all-reduce.2.cloned.1.call-done), kind=kOutput, calls=%fused_computation.63 | convolution fusion | flops 7062945792 | bytes 24134656 | tf_op jit(solution)/shard_map/dot_general | solution.py:133
  336.3 38.7 %all-gather.11.cloned.1.call-done = bf16[3584,1280]{1,0:T(8,128)(2,1)} async-done(((bf16[896,1280]{1,0:T(8,128)(2,1)}), bf16[3584,1280]{1,0:T(8,128)(2,1)}) %all-gather.11.cloned.1.call-update) | async-done | bytes 9175056 | tf_op jit(solution)/shard_map/all_gather | solution.py:95
  375.0 64.3 %all-gather.9.cloned.1.call-done = bf16[3584,1280]{1,0:T(8,128)(2,1)} async-done(((bf16[896,1280]{1,0:T(8,128)(2,1)}), bf16[3584,1280]{1,0:T(8,128)(2,1)}) %all-gather.9.cloned.1.call-update) | async-done | bytes 9175056 | tf_op jit(solution)/shard_map/all_gather | solution.py:94
  439.3 25.9 %convolution_convert_fusion = bf16[768,3584]{1,0:T(8,128)(2,1)} fusion(bf16[3584,1280]{1,0:T(8,128)(2,1)} %all-gather.11.cloned.1.call-done, bf16[3584,1280]{1,0:T(8,128)(2,1)} %all-gather.9.cloned.1.call-done, f32[768,1280]{1,0:T(8,128)} %fusion.33, f32[3584]{0:T(1024)S(1)} %copy-done.12, f32[768]{0:T(1024)S(1)} %add_rsqrt_fusion, ...), kind=kOutput, calls=%fused_computation.12 | convolution fusion | flops 14118027264 | bytes 38814720 | tf_op jit(solution)/shard_map/dot_general | solution.py:55
  466.1 105.5 %reduce-scatter.5.cloned.1.call-done = bf16[96,3584]{1,0:T(8,128)(2,1)} async-done(((bf16[768,3584]{1,0:T(8,128)(2,1)}), bf16[96,3584]{1,0:T(8,128)(2,1)}) %reduce-scatter.5.cloned.1.call-update) | async-done | bytes 688144 | tf_op jit(solution)/shard_map/reduce_scatter | solution.py:146
  571.7 2.2 convolution_convert_fusion.2
  573.9 1.3 copy.39
  575.4 62.5 %reduce-scatter.7.cloned.1.call-done = bf16[448,16]{1,0:T(8,128)(2,1)} async-done(((bf16[3584,16]{1,0:T(8,128)(2,1)}), bf16[448,16]{1,0:T(8,128)(2,1)}) %reduce-scatter.7.cloned.1.call-update) | async-done | bytes 14352
  638.0 1.0 copy.40
  639.1 6.4 all_to_all.5
  (67 shorter events, 8.8 us)
Async XLA Ops:
  6.5 5.4 copy-start.4
  6.5 13.7 %copy-start.8 = (f32[3584]{0:T(1024)S(1)}, f32[3584]{0:T(1024)}, u32[]{:S(2)}) copy-start(f32[3584]{0:T(1024)} %param.15) | copy-start | bytes 43012
  6.5 98.7 %all-gather.5.cloned.1.call-start = ((), (), s32[]{:S(2)}) async-start(), calls=%async_computation.3 | async-start | bytes 2293760 | tf_op jit(solution)/shard_map/all_gather | solution.py:89
  7.3 107.6 %all-gather.7.cloned.1.call-start = ((), (), s32[]{:S(2)}) async-start(), calls=%async_computation.4 | async-start | bytes 2293760 | tf_op jit(solution)/shard_map/all_gather | solution.py:92
  8.0 303.7 %all-reduce.2.cloned.1.call-start = ((), (), s32[]{:S(2)}) async-start(), calls=%async_computation.5 | async-start | bytes 11010048 | tf_op jit(solution)/shard_map/psum | solution.py:130
  8.1 12.2 %copy-start = (bf16[768,3584]{1,0:T(8,128)(2,1)S(1)}, bf16[768,3584]{1,0:T(8,128)(2,1)}, u32[]{:S(2)}) copy-start(bf16[768,3584]{1,0:T(8,128)(2,1)} %param.12) | copy-start | bytes 16515076
  22.4 2.4 copy-start.1
  24.8 34.5 %copy-start.5 = (bf16[896,64]{0,1:T(8,128)(2,1)S(1)}, bf16[896,64]{0,1:T(8,128)(2,1)}, u32[]{:S(2)}) copy-start(bf16[896,64]{0,1:T(8,128)(2,1)} %param.17) | copy-start | bytes 344068
  59.4 44.3 %copy-start.9 = (s32[2,8]{1,0:T(2,128)S(1)}, s32[2,8]{1,0:T(2,128)}, u32[]{:S(2)}) copy-start(s32[2,8]{1,0:T(2,128)} %param.13) | copy-start | bytes 196
  104.4 0.6 copy-start.6
  120.4 1.6 copy-start.3
  120.4 254.6 %all-gather.11.cloned.1.call-start = ((), (), s32[]{:S(2)}) async-start(), calls=%async_computation.7 | async-start | bytes 11468800 | tf_op jit(solution)/shard_map/all_gather | solution.py:95
  121.0 318.3 %all-gather.9.cloned.1.call-start = ((), (), s32[]{:S(2)}) async-start(), calls=%async_computation.6 | async-start | bytes 11468800 | tf_op jit(solution)/shard_map/all_gather | solution.py:94
  121.6 450.1 %reduce-scatter.5.cloned.1.call-start = ((), (), s32[]{:S(2)}) async-start(), calls=%async_computation.8 | async-start | bytes 6193152 | tf_op jit(solution)/shard_map/reduce_scatter | solution.py:146
  122.0 4.6 collective-permute-start
  133.5 101.5 %collective-permute-start.1 = (bf16[2,896,1280]{2,1,0:T(8,128)(2,1)}, bf16[2,896,1280]{2,1,0:T(8,128)(2,1)}, u32[]{:S(2)}, u32[]{:S(2)}) collective-permute-start(bf16[2,896,1280]{2,1,0:T(8,128)(2,1)} %get-tuple-element.8), channel_id=1, source_target_pairs={{0,16},{8,24},{16,0},{24,8},{1,17},{9,25},{17,1},{25,9},{2,18},{10... | collective-permute-start | bytes 13762568 | tf_op jit(solution)/shard_map/ppermute | solution.py:29
  256.4 67.0 %copy-start.12 = (f32[3584]{0:T(1024)S(1)}, f32[3584]{0:T(1024)}, u32[]{:S(2)}) copy-start(f32[3584]{0:T(1024)} %param.20) | copy-start | bytes 43012
  311.7 11.6 %copy-start.2 = (bf16[2,2,896,1280]{3,2,1,0:T(8,128)(2,1)S(1)}, bf16[2,2,896,1280]{3,2,1,0:T(8,128)(2,1)}, u32[]{:S(2)}) copy-start(bf16[2,2,896,1280]{3,2,1,0:T(8,128)(2,1)} %reverse_select_fusion) | copy-start | bytes 27525124
  465.2 0.7 copy-start.7
  465.2 0.8 copy-start.11
  465.2 110.1 %copy-start.10 = (s32[2,8]{1,0:T(2,128)S(1)}, s32[2,8]{1,0:T(2,128)}, u32[]{:S(2)}) copy-start(s32[2,8]{1,0:T(2,128)} %param.13) | copy-start | bytes 196
  465.2 172.7 %reduce-scatter.7.cloned.1.call-start = ((), (), s32[]{:S(2)}) async-start(), calls=%async_computation.9 | async-start | bytes 1032192
Sparse Core Ops, SparseCore 0:
  8.9 23.8 all-gather.4
  34.3 21.1 all-gather.6
  120.5 191.1 all-reduce.1
  313.2 61.7 all-gather.10
  376.5 62.7 all-gather.8
  465.4 106.2 reduce-scatter.4
  575.3 62.6 reduce-scatter.6
